TPU v7x, 256 devices: a whole 4x4x8 slice. The times are simulated.
256 devices in a mesh: req: 64 (over z, x, core), tp: 4 (over y).
Axes of the slice: x: 4, y: 4, z: 8, core: 2. Of those that a mesh axis runs over, the one named last changes fastest.
Arguments:
- layer_in: bfloat16 [8192, 2880], P('req', 'tp'), may hold values from -6 to 6
- queries: bfloat16 [8192, 4096], P('req', 'tp'), may hold values from -32 to 32
- key_values: bfloat16 [8192, 2, 512], P('req', None, 'tp'), may hold values from -12 to 12
- prefix_cache: bfloat16 [4, 1024, 2, 512], P(None, 'req', None, 'tp'), may hold values from -8 to 8
- sink_logits: float32 [64], P('tp'), may hold values from 8 to 12
- lengths: int32 [512], P('req'), may hold values from 1 to 16
- groups: int32 [512], P('req'), may hold values from 0 to 3
- batch_home: int32 [64], replicated, may hold values from 0 to 63, each once
- expert_ids: int32 [8192, 4], P('req'), may hold values from 0 to 31, all different within a row; in each aligned block of 128 rows (0 to 127, 128 to 255, ...) at most 24 rows name the same one
- router_logits: float32 [8192, 4], P('req'), may hold values from -6 to 6
- norm_gain: float32 [2880], replicated, may hold values from 0.1 to 1.9
- output_weight: bfloat16 [4096, 2880], P('tp'), may hold values from -0.09375 to 0.09375
- gate_up: bfloat16 [64, 2880, 2, 1440], P('req', None, None, 'tp'), may hold values from -0.109375 to 0.109375
- expert_down: bfloat16 [64, 1440, 2880], P('req', 'tp'), may hold values from -0.109375 to 0.109375
Outputs:
- layer_out: bfloat16 [8192, 2880], P('req', 'tp')
Inputs may be any that keep to these rules, and one draw needn't show every extreme that they name: `expert_ids`: in the token slots of one index of req, no expert is named by more than 24 slots. `batch_home`: A permutation.
All inputs are finite; a program needn't handle non-finite values.
Results may differ from a plain program's by a relative error of at most 0.017.
Values may be sent and summed in bfloat16 or wider, within the bound.
No kernel may reach another device: no remote copies, remote signals or barrier semaphores. Data moves between devices by JAX's collectives and lax.ppermute only.
A program may use at most 192 MiB of HBM per device.

v0:
```python
import jax
import jax.numpy as jnp
from jax import lax
from jax.sharding import Mesh, PartitionSpec as P

D = 2880
HD = 64
EXPERTS = 32
TOPK = 4
PREFIX = 1024
CAP = 24


theta_base = 150000.0
norm_eps = 1e-05
logit_scale = 0.125
masked_score = -1e30


def rotate(values, positions):
    middle = values.shape[-1] // 2
    lane_index = jnp.arange(middle, dtype=jnp.int32).astype(jnp.float32)
    inverse_freq = theta_base ** (-2.0 * lane_index / values.shape[-1])
    angles = positions.astype(jnp.float32)[:, None] * inverse_freq[None, :]
    cosine = jnp.cos(angles)[:, None, :]
    sine_part = jnp.sin(angles)[:, None, :]
    front_half = values[..., :middle]
    back_half = values[..., middle:]
    return jnp.concatenate(
        [front_half * cosine - back_half * sine_part, back_half * cosine + front_half * sine_part],
        axis=-1,
    )


def body(
    layer_in,
    queries,
    key_values,
    prefix_cache,
    sink_logits,
    lengths,
    groups,
    batch_home,
    expert_ids,
    router_logits,
    norm_gain,
    output_weight,
    gate_up,
    expert_down,
):
    tokens = queries.shape[0]
    requests = lengths.shape[0]
    suffix = tokens // requests
    local_heads = sink_logits.shape[0]
    kv_local = key_values.shape[2] // HD
    per_group = local_heads // kv_local
    slot_index = jnp.tile(jnp.arange(suffix, dtype=jnp.int32), requests)
    positions = PREFIX + slot_index
    rotated_queries = rotate(
        queries.reshape(tokens, local_heads, HD).astype(jnp.float32), positions
    ).astype(jnp.bfloat16)
    query_groups = rotated_queries.reshape(requests, suffix, kv_local, per_group, HD)
    fresh_keys = rotate(
        key_values[:, 0].reshape(tokens, kv_local, HD).astype(jnp.float32), positions
    ).astype(jnp.bfloat16)
    fresh_keys = fresh_keys.reshape(requests, suffix, kv_local, HD)
    fresh_values = key_values[:, 1].reshape(requests, suffix, kv_local, HD)
    sink_values = sink_logits.reshape(kv_local, per_group)
    n_chips = lax.axis_size("chip")
    partner = [(0, 1), (1, 0)]
    page_copies = jnp.broadcast_to(prefix_cache[None], (n_chips,) + prefix_cache.shape)
    pages_same_core = lax.all_to_all(page_copies, "chip", 0, 0, tiled=True)
    pages_other_core = lax.ppermute(pages_same_core, "core", partner)
    page_shards = jnp.concatenate([pages_same_core, pages_other_core], axis=0)
    shard_count, group_count, shard_rows = page_shards.shape[:3]
    span_rows = shard_count * shard_rows
    pages_t = (
        page_shards.reshape(shard_count, group_count, shard_rows, 2, kv_local, HD)
        .transpose(1, 3, 4, 0, 2, 5)
        .reshape(group_count, 2, kv_local, span_rows, HD)
    )
    chosen = pages_t[groups]
    prefix_keys = chosen[:, 0]
    prefix_values = chosen[:, 1]
    prefix_scores = (
        jnp.einsum(
            "rskgd,rkbd->rskgb", query_groups, prefix_keys, preferred_element_type=jnp.float32
        )
        * logit_scale
    )
    local_pos = jnp.arange(suffix, dtype=jnp.int32)
    causal = local_pos[None, :] <= local_pos[:, None]
    within = local_pos[None, None, :] < lengths[:, None, None]
    allowed = (causal[None] & within)[:, :, None, None, :]
    suffix_scores = (
        jnp.einsum(
            "rskgd,rbkd->rskgb", query_groups, fresh_keys, preferred_element_type=jnp.float32
        )
        * logit_scale
    )
    suffix_scores = jnp.where(allowed, suffix_scores, masked_score)
    top_score = jnp.maximum(
        jnp.maximum(jnp.max(prefix_scores, axis=-1), jnp.max(suffix_scores, axis=-1)),
        sink_values[None, None],
    )
    prefix_weights = jnp.exp(prefix_scores - top_score[..., None])
    suffix_weights = jnp.exp(suffix_scores - top_score[..., None])
    totals = (
        jnp.sum(prefix_weights, axis=-1)
        + jnp.sum(suffix_weights, axis=-1)
        + jnp.exp(sink_values[None, None] - top_score)
    )
    value_acc = jnp.einsum(
        "rskgb,rkbd->rskgd",
        prefix_weights.astype(jnp.bfloat16),
        prefix_values,
        preferred_element_type=jnp.float32,
    ) + jnp.einsum(
        "rskgb,rbkd->rskgd",
        suffix_weights.astype(jnp.bfloat16),
        fresh_values,
        preferred_element_type=jnp.float32,
    )
    attention = (
        (value_acc / totals[..., None]).reshape(tokens, local_heads * HD).astype(jnp.bfloat16)
    )
    n_tp = lax.axis_size("tp")
    tp_index = lax.axis_index("tp")
    core = lax.axis_index("core")
    chip = lax.axis_index("chip")
    quarter_cols = D // n_tp
    out_chunks = output_weight.reshape(output_weight.shape[0], n_tp, quarter_cols)
    partial_value = jnp.einsum(
        "nh,htd->tnd", attention, out_chunks, preferred_element_type=jnp.float32
    )
    own_chunk = (jnp.arange(n_tp, dtype=jnp.int32) == tp_index)[:, None, None]
    placed = jnp.where(own_chunk, layer_in.astype(jnp.float32)[None], 0.0)
    residual = lax.psum_scatter(partial_value + placed, "tp", scatter_dimension=0, tiled=True)[
        0
    ].astype(jnp.bfloat16)
    live_rows = slot_index < jnp.repeat(lengths, suffix)
    pair_weight = jnp.where(live_rows[:, None], jax.nn.softmax(router_logits, axis=-1), 0.0).astype(
        jnp.bfloat16
    )
    flat_ids = expert_ids.reshape(-1)
    onehot = (flat_ids[:, None] == jnp.arange(EXPERTS, dtype=jnp.int32)[None, :]).astype(jnp.int32)
    before = jnp.cumsum(onehot, axis=0) - onehot
    rank_in = jnp.sum(before * onehot, axis=1)
    flat_slot = flat_ids * CAP + rank_in
    pair_token = jnp.arange(tokens * TOPK, dtype=jnp.int32) // TOPK
    token_table = (
        jnp.full((EXPERTS * CAP,), tokens, dtype=jnp.int32)
        .at[flat_slot]
        .set(pair_token)
        .reshape(EXPERTS, CAP)
    )
    weight_table = (
        jnp.zeros((EXPERTS * CAP,), jnp.float32)
        .at[flat_slot]
        .set(pair_weight.reshape(-1).astype(jnp.float32))
        .reshape(EXPERTS, CAP)
    )
    meta_send = jnp.stack([token_table.astype(jnp.float32), weight_table], axis=-1)
    meta_all = lax.all_gather(
        meta_send.astype(jnp.bfloat16).reshape(-1), ("chip", "core"), axis=0, tiled=False
    ).reshape((2 * n_chips,) + meta_send.shape)
    padded = jnp.concatenate([residual, jnp.zeros((1, quarter_cols), jnp.bfloat16)], axis=0)
    rows_send = padded[token_table]
    rows_own = lax.all_to_all(rows_send, "chip", 0, 0, tiled=True)
    rows_gathered = lax.all_gather(rows_own, "tp", axis=0, tiled=False)
    meta_all, rows_gathered = lax.optimization_barrier((meta_all, rows_gathered))
    rows_other = lax.ppermute(rows_gathered, "core", partner)
    all_rows = jnp.where(
        core == 0,
        jnp.concatenate([rows_gathered, rows_other], axis=1),
        jnp.concatenate([rows_other, rows_gathered], axis=1),
    )
    chip_range = jnp.arange(n_chips, dtype=jnp.int32)
    source_of = jnp.concatenate([2 * chip_range, 2 * chip_range + 1])
    all_meta = meta_all[source_of, chip]
    slab_rows = all_rows.shape[1] * all_rows.shape[2]
    rows_q = all_rows.reshape(n_tp, slab_rows, quarter_cols)
    rows_float = rows_q.astype(jnp.float32)
    row_scale = lax.rsqrt(
        jnp.mean(rows_float * rows_float, axis=(0, 2), keepdims=True) + norm_eps
    )
    gain_q = norm_gain.reshape(n_tp, 1, quarter_cols)
    normed = (rows_float * row_scale * gain_q).astype(jnp.bfloat16)
    gate_q = gate_up[0].reshape(n_tp, quarter_cols, 2, gate_up.shape[3])
    gate_and_up = jnp.einsum(
        "tnd,tdgf->ngf", normed, gate_q, preferred_element_type=jnp.float32
    )
    hidden = (jax.nn.silu(gate_and_up[:, 0, :]) * gate_and_up[:, 1, :]).astype(jnp.bfloat16)
    half_cols = quarter_cols // 2
    down_chunks = expert_down[0].reshape(expert_down.shape[1], n_tp, 2, half_cols)
    partial_out = jnp.einsum(
        "nf,fthd->htnd", hidden, down_chunks, preferred_element_type=jnp.float32
    ).astype(jnp.bfloat16)
    half_keep = lax.dynamic_index_in_dim(partial_out, core, 0, keepdims=False)
    half_send = lax.dynamic_index_in_dim(partial_out, 1 - core, 0, keepdims=False)
    half_recv = lax.ppermute(half_send, "core", partner)
    pair_sum = (half_keep.astype(jnp.float32) + half_recv.astype(jnp.float32)).astype(
        jnp.bfloat16
    )
    value_total = lax.psum_scatter(pair_sum, "tp", scatter_dimension=0, tiled=True)[0].astype(
        jnp.float32
    )
    own_rows = lax.dynamic_index_in_dim(rows_q, tp_index, 0, keepdims=False)
    own_half = lax.dynamic_index_in_dim(
        own_rows.reshape(slab_rows, 2, half_cols), core, 1, keepdims=False
    ).astype(jnp.float32)
    row_weight = all_meta[..., 1].astype(jnp.float32).reshape(slab_rows)
    result = (row_weight[:, None] * (value_total + own_half)).astype(jnp.bfloat16)
    result = result.reshape(all_meta.shape[0], all_meta.shape[1], half_cols)
    devices_req = 2 * n_chips
    device_range = jnp.arange(devices_req, dtype=jnp.int32)
    inverse = jnp.sum(
        device_range[:, None] * (batch_home[:, None] == device_range[None, :]).astype(jnp.int32),
        axis=0,
    )
    local_of = (inverse % 2) * n_chips + inverse // 2
    sent = result[local_of]
    returned = lax.all_to_all(sent, ("chip", "core"), 0, 0, tiled=True)
    home_batch = inverse[2 * chip + core]
    flat_rows = (
        returned.reshape(n_chips, 2, all_meta.shape[1], half_cols)
        .transpose(0, 2, 1, 3)
        .reshape(-1, quarter_cols)
    )
    flat_token = meta_all[home_batch, :, :, 0].reshape(-1).astype(jnp.int32)
    selector = (jnp.arange(tokens, dtype=jnp.int32)[:, None] == flat_token[None, :]).astype(
        jnp.bfloat16
    )
    return jnp.dot(selector, flat_rows, preferred_element_type=jnp.float32).astype(jnp.bfloat16)


def solution(mesh):
    req = ("chip", "core")
    n_req, n_tp = mesh.devices.shape
    split_mesh = Mesh(mesh.devices.reshape(n_req // 2, 2, n_tp), ("chip", "core", "tp"))
    placed = (
        P(req, "tp"),
        P(req, "tp"),
        P(req, None, "tp"),
        P(None, req, None, "tp"),
        P("tp"),
        P(req),
        P(req),
        P(),
        P(req, None),
        P(req, None),
        P(),
        P("tp", None),
        P(req, None, None, "tp"),
        P(req, "tp", None),
    )
    return jax.shard_map(
        body, mesh=split_mesh, in_specs=placed, out_specs=P(req, "tp"), check_vma=False
    )
```

profile of v0, /device:TPU:2, one launch (start us, length us, event | category | flops | bytes accessed | tf_op | source)
XLA Modules:
  0.0 389.6 jit_solution(2609455193026399372)
XLA Ops:
  8.6 11.7 %all-to-all-start = ((bf16[32,4,16,2,128]{4,2,3,1,0:T(8,128)(2,1)}), bf16[32,4,16,2,128]{4,2,3,1,0:T(8,128)(2,1)S(1)}, u32[]{:S(2)}, u32[]{:S(2)}) async-start(bf16[32,4,16,2,128]{4,2,3,1,0:T(8,128)(2,1)} %broadcast_in_dim.55), calls=%async_computation | async-start | bytes 2097152 | tf_op jit(solution)/shard_map/all_to_all | solution.py:72
  23.2 25.2 %all-to-all-done = bf16[32,4,16,2,128]{4,2,3,1,0:T(8,128)(2,1)S(1)} async-done(((bf16[32,4,16,2,128]{4,2,3,1,0:T(8,128)(2,1)}), bf16[32,4,16,2,128]{4,2,3,1,0:T(8,128)(2,1)S(1)}, u32[]{:S(2)}, u32[]{:S(2)}) %all-to-all-start) | async-done | bytes 1048608 | tf_op jit(solution)/shard_map/all_to_all | solution.py:72
  51.1 3.1 fusion.63
  56.0 3.3 reshape.468
  59.3 5.0 %copy.132 = bf16[4,2,2,64,16,64]{5,4,3,2,1,0:T(8,128)(2,1)} copy(bf16[4,2,2,64,16,64]{5,2,4,1,0,3:T(2,128)(2,1)} %bitcast.169) | data formatting | bytes 4194304 | tf_op jit(solution)/shard_map/transpose | solution.py:79
  64.2 3.5 copy.133
  70.5 3.1 bitcast_reduce_fusion
  78.9 5.5 %bitcast_add_fusion.1 = f32[4,128,720]{1,2,0:T(8,128)} fusion(bf16[128,1024,1]{1,0,2:T(8,128)(2,1)S(1)} %reshape.539, bf16[1024,4,720]{0,2,1:T(8,128)(2,1)} %bitcast.175, f32[128,720]{0,1:T(8,128)S(1)} %convert_element_type.230, pred[4]{0:T(512)(128)(4,1)S(1)} %iota_compare_fusion.7), kind=kOutput, calls=%fused_computation.34 | convolution fusion | flops 755712000 | bytes 8003588 | tf_op jit(solution)/shard_map/nh,htd->tnd/dot_general | solution.py:133
  89.6 19.7 %reduce-scatter.3.cloned.1.call-done = f32[1,128,720]{1,2,0:T(8,128)} async-done(((f32[4,128,720]{1,2,0:T(8,128)}), f32[1,128,720]{1,2,0:T(8,128)}) %reduce-scatter.3.cloned.1.call-update) | async-done | bytes 368656 | tf_op jit(solution)/shard_map/reduce_scatter | solution.py:138
  113.3 39.8 %all_to_all.15 = bf16[32,24,720]{2,1,0:T(8,128)(2,1)} all-to-all(bf16[32,24,720]{2,1,0:T(8,128)(2,1)S(1)} %bitcast.179), channel_id=1, replica_groups=mesh['chip'=32,'core'=2,'tp'=4] {'chip'}, dimensions={0} | all-to-all | bytes 2211840 | tf_op jit(solution)/shard_map/all_to_all | solution.py:169
  156.7 46.5 %all-gather.1 = bf16[64,1,1536]{2,1,0:T(2,128)(2,1)S(1)} all-gather(bf16[1,1,1536]{2,1,0:T(2,128)(2,1)S(1)} %reshape.531), channel_id=1, replica_groups=mesh['chip'=32,'core'=2,'tp'=4] {'chip','core'}, dimensions={0}, use_global_device_ids=true | all-gather | bytes 199680 | tf_op jit(solution)/shard_map/all_gather | solution.py:164
  204.2 3.4 copy.173
  207.6 11.1 %reshape_squeeze.12 = bf16[4,720,2,360]{1,0,3,2:T(4,128)(2,1)} reshape(bf16[1,2880,2,360]{1,3,2,0:T(8,128)(2,1)} %param.26) | data formatting | bytes 8294400 | tf_op jit(solution)/shard_map/reshape;squeeze | solution.py:189
  218.6 13.0 %multiply_reduce_fusion = (f32[64,24]{1,0:T(8,128)S(1)}, bf16[4,64,24,720]{3,2,1,0:T(8,128)(2,1)}) fusion(bf16[4,32,24,720]{3,2,1,0:T(8,128)(2,1)} %bitcast.181, bf16[4,32,24,720]{3,2,1,0:T(8,128)(2,1)} %collective-permute-done.1, pred[]{:T(512)S(6)} %eq.82), kind=kLoop, calls=%fused_computation.7 | loop fusion | flops 26540544 | bytes 17700864 | tf_op jit(solution)/shard_map/reduce_sum | solution.py:185
  231.7 11.4 %fusion.14 = f32[1536,2,360]{0,2,1:T(8,128)S(1)} fusion(bf16[4,720,2,360]{1,0,3,2:T(4,128)(2,1)} %reshape_squeeze.12, bf16[4,1536,720]{2,1,0:T(8,128)(2,1)} %bitcast.171, f32[4,720]{1,0:T(4,128)S(1)} %mul.300, f32[1536]{0:T(1024)S(1)} %rsqrt.12), kind=kOutput, calls=%fused_computation.26 | convolution fusion | flops 6387793920 | bytes 17435904 | tf_op jit(solution)/shard_map/tnd,tdgf->ngf/dot_general | solution.py:190
  243.1 5.2 %convolution_convert_fusion = bf16[1536,4,2,360]{0,3,2,1:T(8,128)(2,1)S(1)} fusion(bf16[360,4,2,360]{0,3,2,1:T(8,128)(2,1)S(1)} %bitcast.184, f32[1536,2,360]{0,2,1:T(8,128)S(1)} %fusion.14), kind=kOutput, calls=%fused_computation.20 | convolution fusion | flops 3192791040 | bytes 15344640 | tf_op jit(solution)/shard_map/nf,fthd->htnd/dot_general | solution.py:196
  253.1 11.8 %collective-permute-start.2 = (bf16[4,1536,360]{1,2,0:T(8,128)(2,1)}, bf16[4,1536,360]{1,2,0:T(8,128)(2,1)}, u32[]{:S(2)}, u32[]{:S(2)}) collective-permute-start(bf16[4,1536,360]{1,2,0:T(8,128)(2,1)} %dynamic-slice_bitcast_fusion), channel_id=1, source_target_pairs={{0,4},{4,0},{1,5},{5,1},{2,6},{6,2},{3,7},{7,3},{8,12},{12,8},{9,1... | collective-permute-start | bytes 13271048 | tf_op jit(solution)/shard_map/ppermute | solution.py:201
  264.9 7.5 %collective-permute-done.2 = bf16[4,1536,360]{1,2,0:T(8,128)(2,1)} collective-permute-done((bf16[4,1536,360]{1,2,0:T(8,128)(2,1)}, bf16[4,1536,360]{1,2,0:T(8,128)(2,1)}, u32[]{:S(2)}, u32[]{:S(2)}) %collective-permute-start.2) | collective-permute-done | bytes 4423712 | tf_op jit(solution)/shard_map/ppermute | solution.py:201
  272.4 6.9 %fusion.5 = bf16[4,1536,360]{1,2,0:T(8,128)(2,1)} fusion(bf16[4,1536,360]{1,2,0:T(8,128)(2,1)} %collective-permute-done.2, bf16[1536,4,2,360]{0,3,2,1:T(8,128)(2,1)} %copy-done.1, s32[]{:T(128)S(6)} %select_n.136), kind=kLoop, calls=%fused_computation.14 | loop fusion | flops 8847360 | bytes 13271044 | tf_op jit(solution)/shard_map/convert_element_type | solution.py:202
  286.9 2.9 dynamic-slice_convert_fusion
  291.8 39.4 %reduce-scatter.5.cloned.1.call-done = bf16[1,1536,360]{1,2,0:T(8,128)(2,1)} async-done(((bf16[4,1536,360]{1,2,0:T(8,128)(2,1)}), bf16[1,1536,360]{1,2,0:T(8,128)(2,1)}) %reduce-scatter.5.cloned.1.call-update) | async-done | bytes 1105936 | tf_op jit(solution)/shard_map/reduce_scatter | solution.py:205
  337.6 10.5 %all-to-all-start.2 = ((bf16[64,24,360]{2,1,0:T(8,128)(2,1)}), bf16[64,24,360]{2,1,0:T(8,128)(2,1)S(1)}, u32[]{:S(2)}, u32[]{:S(2)}) async-start(bf16[64,24,360]{2,1,0:T(8,128)(2,1)} %gather_fusion.3), calls=%async_computation.4 | async-start | bytes 2359296 | tf_op jit(solution)/shard_map/all_to_all | solution.py:223
  350.7 14.4 %convert_reduce_fusion = s32[32,24]{1,0:T(8,128)S(1)} fusion(bf16[64,32,24,2]{0,3,2,1:T(2,128)(2,1)S(1)} %bitcast.183, s32[]{:T(128)S(6)} %select_n.130), kind=kLoop, calls=%fused_computation.52 | loop fusion | flops 768 | bytes 4612 | tf_op jit(solution)/shard_map/convert_element_type | solution.py:230
  365.1 14.6 %all-to-all-done.2 = bf16[64,24,360]{2,1,0:T(8,128)(2,1)S(1)} async-done(((bf16[64,24,360]{2,1,0:T(8,128)(2,1)}), bf16[64,24,360]{2,1,0:T(8,128)(2,1)S(1)}, u32[]{:S(2)}, u32[]{:S(2)}) %all-to-all-start.2) | async-done | bytes 1105952 | tf_op jit(solution)/shard_map/all_to_all | solution.py:223
  (140 shorter events, 55.3 us)
Async XLA Ops:
  6.5 41.9 %copy-start.12 = (f32[16]{0:T(128)S(1)}, f32[16]{0:T(128)}, u32[]{:S(2)}) copy-start(f32[16]{0:T(128)} %param.18) | copy-start | bytes 196
  6.5 43.2 %copy-start.7 = (bf16[128,720]{0,1:T(8,128)(2,1)S(1)}, bf16[128,720]{0,1:T(8,128)(2,1)}, u32[]{:S(2)}) copy-start(bf16[128,720]{0,1:T(8,128)(2,1)} %param.14) | copy-start | bytes 552964
  8.6 42.3 %copy-start.13 = (s32[8]{0:T(128)S(1)}, s32[8]{0:T(128)}, u32[]{:S(2)}) copy-start(s32[8]{0:T(128)} %param.20) | copy-start | bytes 100
  8.6 42.4 %copy-start.14 = (s32[8]{0:T(128)S(1)}, s32[8]{0:T(128)}, u32[]{:S(2)}) copy-start(s32[8]{0:T(128)} %param.19) | copy-start | bytes 100
  8.6 39.8 %all-to-all-start = ((bf16[32,4,16,2,128]{4,2,3,1,0:T(8,128)(2,1)}), bf16[32,4,16,2,128]{4,2,3,1,0:T(8,128)(2,1)S(1)}, u32[]{:S(2)}, u32[]{:S(2)}) async-start(bf16[32,4,16,2,128]{4,2,3,1,0:T(8,128)(2,1)} %broadcast_in_dim.55), calls=%async_computation | async-start | bytes 2097152 | tf_op jit(solution)/shard_map/all_to_all | solution.py:72
  20.3 89.0 %reduce-scatter.3.cloned.1.call-start = ((), (), s32[]{:S(2)}) async-start(), calls=%async_computation.5 | async-start | bytes 1843200 | tf_op jit(solution)/shard_map/reduce_scatter | solution.py:138
  48.4 5.8 %copy-start.3 = (bf16[32,4,16,2,128]{4,2,3,1,0:T(8,128)(2,1)}, bf16[32,4,16,2,128]{4,2,3,1,0:T(8,128)(2,1)S(1)}, u32[]{:S(2)}) copy-start(bf16[32,4,16,2,128]{4,2,3,1,0:T(8,128)(2,1)S(1)} %all-to-all-done) | copy-start | bytes 3145732
  48.4 5.8 %collective-permute-start = (bf16[32,4,16,2,128]{4,2,3,1,0:T(8,128)(2,1)S(1)}, bf16[32,4,16,2,128]{4,2,3,1,0:T(8,128)(2,1)}, u32[]{:S(2)}, u32[]{:S(2)}) collective-permute-start(bf16[32,4,16,2,128]{4,2,3,1,0:T(8,128)(2,1)S(1)} %all-to-all-done), channel_id=1, source_target_pairs={{0,4},{4,0},{1,5},{5,1},{2,6},{6,2},{3,7},{7,3},{8,12},{12,8},{9,1... | collective-permute-start | bytes 3145736 | tf_op jit(solution)/shard_map/ppermute | solution.py:73
  70.5 3.1 copy-start.6
  70.5 3.2 copy-start
  75.5 1.9 copy-start.2
  75.5 2.3 copy-start.8
  78.9 5.6 %copy-start.11 = (s32[128,4]{0,1:T(4,128)S(1)}, s32[128,4]{0,1:T(4,128)}, u32[]{:S(2)}) copy-start(s32[128,4]{0,1:T(4,128)} %param.22) | copy-start | bytes 6148
  84.5 119.5 %all-gather.4.cloned.1.call-start = ((), (), s32[]{:S(2)}) async-start(), calls=%async_computation.7 | async-start | bytes 5898240 | tf_op jit(solution)/shard_map/all_gather | solution.py:170
  110.5 42.8 %copy-start.9 = (f32[128,4]{0,1:T(4,128)S(1)}, f32[128,4]{0,1:T(4,128)}, u32[]{:S(2)}) copy-start(f32[128,4]{0,1:T(4,128)} %param.23) | copy-start | bytes 6148
  113.3 90.8 %copy-start.10 = (f32[2880]{0:T(1024)S(1)}, f32[2880]{0:T(1024)}, u32[]{:S(2)}) copy-start(f32[2880]{0:T(1024)} %param.24) | copy-start | bytes 34564
  153.1 178.0 %reduce-scatter.5.cloned.1.call-start = ((), (), s32[]{:S(2)}) async-start(), calls=%async_computation.6 | async-start | bytes 5529600 | tf_op jit(solution)/shard_map/reduce_scatter | solution.py:205
  203.6 76.4 %copy-start.4 = (bf16[64,1,1536]{0,2,1:T(8,128)(2,1)}, bf16[64,1,1536]{0,2,1:T(8,128)(2,1)S(1)}, u32[]{:S(2)}) copy-start(bf16[64,1,1536]{0,2,1:T(8,128)(2,1)S(1)} %copy.130) | copy-start | bytes 589828
  203.9 14.7 %collective-permute-start.1 = (bf16[4,32,24,720]{3,2,1,0:T(8,128)(2,1)}, bf16[4,32,24,720]{3,2,1,0:T(8,128)(2,1)}, u32[]{:S(2)}, u32[]{:S(2)}) collective-permute-start(bf16[4,32,24,720]{3,2,1,0:T(8,128)(2,1)} %bitcast.180), channel_id=1, source_target_pairs={{0,4},{4,0},{1,5},{5,1},{2,6},{6,2},{3,7},{7,3},{8,12},{12,8},{9,1... | collective-permute-start | bytes 13271048 | tf_op jit(solution)/shard_map/ppermute | solution.py:172
  248.4 4.8 %copy-start.1 = (bf16[1536,4,2,360]{0,3,2,1:T(8,128)(2,1)}, bf16[1536,4,2,360]{0,3,2,1:T(8,128)(2,1)S(1)}, u32[]{:S(2)}) copy-start(bf16[1536,4,2,360]{0,3,2,1:T(8,128)(2,1)S(1)} %convolution_convert_fusion) | copy-start | bytes 26542084
  253.1 19.3 %collective-permute-start.2 = (bf16[4,1536,360]{1,2,0:T(8,128)(2,1)}, bf16[4,1536,360]{1,2,0:T(8,128)(2,1)}, u32[]{:S(2)}, u32[]{:S(2)}) collective-permute-start(bf16[4,1536,360]{1,2,0:T(8,128)(2,1)} %dynamic-slice_bitcast_fusion), channel_id=1, source_target_pairs={{0,4},{4,0},{1,5},{5,1},{2,6},{6,2},{3,7},{7,3},{8,12},{12,8},{9,1... | collective-permute-start | bytes 13271048 | tf_op jit(solution)/shard_map/ppermute | solution.py:201
  279.3 0.7 copy-start.15
  335.8 14.8 %copy-start.5 = (bf16[64,1,1536]{0,2,1:T(8,128)(2,1)S(1)}, bf16[64,1,1536]{0,2,1:T(8,128)(2,1)}, u32[]{:S(2)}) copy-start(bf16[64,1,1536]{0,2,1:T(8,128)(2,1)} %copy-done.4) | copy-start | bytes 589828
  337.6 42.1 %all-to-all-start.2 = ((bf16[64,24,360]{2,1,0:T(8,128)(2,1)}), bf16[64,24,360]{2,1,0:T(8,128)(2,1)S(1)}, u32[]{:S(2)}, u32[]{:S(2)}) async-start(bf16[64,24,360]{2,1,0:T(8,128)(2,1)} %gather_fusion.3), calls=%async_computation.4 | async-start | bytes 2359296 | tf_op jit(solution)/shard_map/all_to_all | solution.py:223
Sparse Core Ops, SparseCore 0:
  84.6 24.6 reduce-scatter.2
  153.3 50.6 all-gather.3
  279.4 51.6 reduce-scatter.4
where the time goes:
time: 395 us; the launch traced here: 390 us
  waiting for transfers between devices  107 us (27%)
  blocking collectives  86.3 us (22%)
  local copies, waits for them, and re-layouts  67.4 us (17%)
  other arithmetic  46.9 us (12%)
  starting transfers between devices  34.4 us (9%)
  matrix products  31.9 us (8%)
  between operations  15.9 us (4%)
    all_gather x1, blocking collectives, body(): lax.all_gather(meta_send.astype(jnp.bfloat16).reshape(-1), ('chip', 'core...  46.5 us
    all_to_all x1, blocking collectives, body(): rows_own = lax.all_to_all(rows_send, 'chip', 0, 0, tiled=True)  39.8 us
    reduce_scatter x1, waiting for transfers between devices, body(): lax.psum_scatter(pair_sum, 'tp', scatter_dimension=0, tiled=True)[0]  39.4 us
    all_to_all x1, waiting for transfers between devices, body(): pages_same_core = lax.all_to_all(page_copies, 'chip', 0, 0, tiled=True)  25.2 us
    reduce_scatter x1, waiting for transfers between devices, body(): lax.psum_scatter(partial_value + placed, 'tp', scatter_dimension=0, tiled...  19.7 us
    all_to_all x1, waiting for transfers between devices, body(): returned = lax.all_to_all(sent, ('chip', 'core'), 0, 0, tiled=True)  14.6 us
    convert_element_type x1, other arithmetic, body(): flat_token = meta_all[home_batch, :, :, 0].reshape(-1).astype(jnp.int32)  14.4 us
    reduce_sum x1, other arithmetic, body(): jnp.mean(rows_float * rows_float, axis=(0, 2), keepdims=True) + norm_eps  13 us
  transfers between devices with their start and end apart: 8, of which 6 were waited for; matrix products, arithmetic and copies ran while one was open for 15% of the time, Pallas kernels for 0%

commit v1 on v0

--- a/solution.py
+++ b/solution.py
@@ -135,9 +135,9 @@
     )
     own_chunk = (jnp.arange(n_tp, dtype=jnp.int32) == tp_index)[:, None, None]
     placed = jnp.where(own_chunk, layer_in.astype(jnp.float32)[None], 0.0)
-    residual = lax.psum_scatter(partial_value + placed, "tp", scatter_dimension=0, tiled=True)[
-        0
-    ].astype(jnp.bfloat16)
+    residual = lax.psum_scatter(
+        (partial_value + placed).astype(jnp.bfloat16), "tp", scatter_dimension=0, tiled=True
+    )[0]
     live_rows = slot_index < jnp.repeat(lengths, suffix)
     pair_weight = jnp.where(live_rows[:, None], jax.nn.softmax(router_logits, axis=-1), 0.0).astype(
         jnp.bfloat16

time: 395 us -> 391 us (0.990)
  waiting for transfers between devices: 107 us -> 103 us
where the time goes in v1:
time: 391 us; the launch traced here: 385 us
  waiting for transfers between devices  103 us (26%)
  blocking collectives  85.5 us (22%)
  local copies, waits for them, and re-layouts  68.6 us (18%)
  other arithmetic  45.9 us (12%)
  starting transfers between devices  34.4 us (9%)
  matrix products  31.7 us (8%)
  between operations  15.9 us (4%)
    all_gather x1, blocking collectives, body(): lax.all_gather(meta_send.astype(jnp.bfloat16).reshape(-1), ('chip', 'core...  46.6 us
    all_to_all x1, blocking collectives, body(): rows_own = lax.all_to_all(rows_send, 'chip', 0, 0, tiled=True)  38.9 us
    reduce_scatter x1, waiting for transfers between devices, body(): lax.psum_scatter(pair_sum, 'tp', scatter_dimension=0, tiled=True)[0]  38.9 us
    all_to_all x1, waiting for transfers between devices, body(): pages_same_core = lax.all_to_all(page_copies, 'chip', 0, 0, tiled=True)  25.2 us
    reduce_scatter x1, waiting for transfers between devices, body(): lax.psum_scatter((partial_value + placed).astype(jnp.bfloat16), 'tp', sca...  17.1 us
    all_to_all x1, waiting for transfers between devices, body(): returned = lax.all_to_all(sent, ('chip', 'core'), 0, 0, tiled=True)  14.6 us
    convert_element_type x1, other arithmetic, body(): flat_token = meta_all[home_batch, :, :, 0].reshape(-1).astype(jnp.int32)  14.4 us
    reduce_sum x1, other arithmetic, body(): jnp.mean(rows_float * rows_float, axis=(0, 2), keepdims=True) + norm_eps  13 us
  transfers between devices with their start and end apart: 8, of which 6 were waited for; matrix products, arithmetic and copies ran while one was open for 15% of the time, Pallas kernels for 0%

profile of v1, /device:TPU:2, one launch (start us, length us, event | category | flops | bytes accessed | tf_op | source)
XLA Modules:
  0.0 385.5 jit_solution(16328765609000335762)
XLA Ops:
  8.6 11.7 %all-to-all-start = ((bf16[32,4,16,2,128]{4,2,3,1,0:T(8,128)(2,1)}), bf16[32,4,16,2,128]{4,2,3,1,0:T(8,128)(2,1)S(1)}, u32[]{:S(2)}, u32[]{:S(2)}) async-start(bf16[32,4,16,2,128]{4,2,3,1,0:T(8,128)(2,1)} %broadcast_in_dim.55), calls=%async_computation | async-start | bytes 2097152 | tf_op jit(solution)/shard_map/all_to_all | solution.py:72
  23.2 25.2 %all-to-all-done = bf16[32,4,16,2,128]{4,2,3,1,0:T(8,128)(2,1)S(1)} async-done(((bf16[32,4,16,2,128]{4,2,3,1,0:T(8,128)(2,1)}), bf16[32,4,16,2,128]{4,2,3,1,0:T(8,128)(2,1)S(1)}, u32[]{:S(2)}, u32[]{:S(2)}) %all-to-all-start) | async-done | bytes 1048608 | tf_op jit(solution)/shard_map/all_to_all | solution.py:72
  51.1 3.1 fusion.64
  56.0 3.3 reshape.467
  59.3 5.0 %copy.132 = bf16[4,2,2,64,16,64]{5,4,3,2,1,0:T(8,128)(2,1)} copy(bf16[4,2,2,64,16,64]{5,2,4,1,0,3:T(2,128)(2,1)} %bitcast.170) | data formatting | bytes 4194304 | tf_op jit(solution)/shard_map/transpose | solution.py:79
  64.2 3.5 copy.133
  70.5 3.1 bitcast_reduce_fusion
  78.9 5.3 %fusion.21 = bf16[4,128,720]{1,2,0:T(8,128)(2,1)} fusion(bf16[128,1024,1]{1,0,2:T(8,128)(2,1)S(1)} %reshape.538, bf16[1024,4,720]{0,2,1:T(8,128)(2,1)} %bitcast.176, f32[128,720]{0,1:T(8,128)S(1)} %convert_element_type.227, pred[4]{0:T(512)(128)(4,1)S(1)} %iota_compare_fusion.7), kind=kOutput, calls=%fused_computation.35 | convolution fusion | flops 756080640 | bytes 7266308 | tf_op jit(solution)/shard_map/nh,htd->tnd/dot_general | solution.py:133
  89.3 17.1 %reduce-scatter.3.cloned.1.call-done = bf16[1,128,720]{1,2,0:T(8,128)(2,1)} async-done(((bf16[4,128,720]{1,2,0:T(8,128)(2,1)}), bf16[1,128,720]{1,2,0:T(8,128)(2,1)}) %reduce-scatter.3.cloned.1.call-update) | async-done | bytes 184336 | tf_op jit(solution)/shard_map/reduce_scatter | solution.py:138
  110.3 38.9 %all_to_all.15 = bf16[32,24,720]{2,1,0:T(8,128)(2,1)} all-to-all(bf16[32,24,720]{2,1,0:T(8,128)(2,1)S(1)} %bitcast.180), channel_id=1, replica_groups=mesh['chip'=32,'core'=2,'tp'=4] {'chip'}, dimensions={0} | all-to-all | bytes 2211840 | tf_op jit(solution)/shard_map/all_to_all | solution.py:169
  152.8 46.6 %all-gather.1 = bf16[64,1,1536]{2,1,0:T(2,128)(2,1)S(1)} all-gather(bf16[1,1,1536]{2,1,0:T(2,128)(2,1)S(1)} %reshape.530), channel_id=1, replica_groups=mesh['chip'=32,'core'=2,'tp'=4] {'chip','core'}, dimensions={0}, use_global_device_ids=true | all-gather | bytes 199680 | tf_op jit(solution)/shard_map/all_gather | solution.py:164
  200.4 3.4 copy.173
  203.7 11.1 %reshape_squeeze.12 = bf16[4,720,2,360]{1,0,3,2:T(4,128)(2,1)} reshape(bf16[1,2880,2,360]{1,3,2,0:T(8,128)(2,1)} %param.26) | data formatting | bytes 8294400 | tf_op jit(solution)/shard_map/reshape;squeeze | solution.py:189
  214.8 13.0 %multiply_reduce_fusion = (f32[64,24]{1,0:T(8,128)S(1)}, bf16[4,64,24,720]{3,2,1,0:T(8,128)(2,1)}) fusion(bf16[4,32,24,720]{3,2,1,0:T(8,128)(2,1)} %bitcast.182, bf16[4,32,24,720]{3,2,1,0:T(8,128)(2,1)} %collective-permute-done.1, pred[]{:T(512)S(6)} %eq.82), kind=kLoop, calls=%fused_computation.7 | loop fusion | flops 26540544 | bytes 17700864 | tf_op jit(solution)/shard_map/reduce_sum | solution.py:185
  227.9 11.4 %fusion.14 = f32[1536,2,360]{0,2,1:T(8,128)S(1)} fusion(bf16[4,720,2,360]{1,0,3,2:T(4,128)(2,1)} %reshape_squeeze.12, bf16[4,1536,720]{2,1,0:T(8,128)(2,1)} %bitcast.172, f32[4,720]{1,0:T(4,128)S(1)} %mul.300, f32[1536]{0:T(1024)S(1)} %rsqrt.12), kind=kOutput, calls=%fused_computation.26 | convolution fusion | flops 6387793920 | bytes 17435904 | tf_op jit(solution)/shard_map/tnd,tdgf->ngf/dot_general | solution.py:190
  239.3 5.2 %convolution_convert_fusion = bf16[1536,4,2,360]{0,3,2,1:T(8,128)(2,1)S(1)} fusion(bf16[360,4,2,360]{0,3,2,1:T(8,128)(2,1)S(1)} %bitcast.185, f32[1536,2,360]{0,2,1:T(8,128)S(1)} %fusion.14), kind=kOutput, calls=%fused_computation.20 | convolution fusion | flops 3192791040 | bytes 15344640 | tf_op jit(solution)/shard_map/nf,fthd->htnd/dot_general | solution.py:196
  249.3 11.6 %collective-permute-start.2 = (bf16[4,1536,360]{1,2,0:T(8,128)(2,1)}, bf16[4,1536,360]{1,2,0:T(8,128)(2,1)}, u32[]{:S(2)}, u32[]{:S(2)}) collective-permute-start(bf16[4,1536,360]{1,2,0:T(8,128)(2,1)} %dynamic-slice_bitcast_fusion), channel_id=1, source_target_pairs={{0,4},{4,0},{1,5},{5,1},{2,6},{6,2},{3,7},{7,3},{8,12},{12,8},{9,1... | collective-permute-start | bytes 13271048 | tf_op jit(solution)/shard_map/ppermute | solution.py:201
  260.9 7.7 %collective-permute-done.2 = bf16[4,1536,360]{1,2,0:T(8,128)(2,1)} collective-permute-done((bf16[4,1536,360]{1,2,0:T(8,128)(2,1)}, bf16[4,1536,360]{1,2,0:T(8,128)(2,1)}, u32[]{:S(2)}, u32[]{:S(2)}) %collective-permute-start.2) | collective-permute-done | bytes 4423712 | tf_op jit(solution)/shard_map/ppermute | solution.py:201
  268.6 6.9 %fusion.5 = bf16[4,1536,360]{1,2,0:T(8,128)(2,1)} fusion(bf16[4,1536,360]{1,2,0:T(8,128)(2,1)} %collective-permute-done.2, bf16[1536,4,2,360]{0,3,2,1:T(8,128)(2,1)} %copy-done.1, s32[]{:T(128)S(6)} %select_n.136), kind=kLoop, calls=%fused_computation.14 | loop fusion | flops 8847360 | bytes 13271044 | tf_op jit(solution)/shard_map/convert_element_type | solution.py:202
  283.0 2.9 dynamic-slice_convert_fusion
  288.2 38.9 %reduce-scatter.5.cloned.1.call-done = bf16[1,1536,360]{1,2,0:T(8,128)(2,1)} async-done(((bf16[4,1536,360]{1,2,0:T(8,128)(2,1)}), bf16[1,1536,360]{1,2,0:T(8,128)(2,1)}) %reduce-scatter.5.cloned.1.call-update) | async-done | bytes 1105936 | tf_op jit(solution)/shard_map/reduce_scatter | solution.py:205
  333.5 10.5 %all-to-all-start.2 = ((bf16[64,24,360]{2,1,0:T(8,128)(2,1)}), bf16[64,24,360]{2,1,0:T(8,128)(2,1)S(1)}, u32[]{:S(2)}, u32[]{:S(2)}) async-start(bf16[64,24,360]{2,1,0:T(8,128)(2,1)} %gather_fusion.3), calls=%async_computation.4 | async-start | bytes 2359296 | tf_op jit(solution)/shard_map/all_to_all | solution.py:223
  346.6 14.4 %convert_reduce_fusion = s32[32,24]{1,0:T(8,128)S(1)} fusion(bf16[64,32,24,2]{0,3,2,1:T(2,128)(2,1)S(1)} %bitcast.184, s32[]{:T(128)S(6)} %select_n.130), kind=kLoop, calls=%fused_computation.53 | loop fusion | flops 768 | bytes 4612 | tf_op jit(solution)/shard_map/convert_element_type | solution.py:230
  361.1 14.6 %all-to-all-done.2 = bf16[64,24,360]{2,1,0:T(8,128)(2,1)S(1)} async-done(((bf16[64,24,360]{2,1,0:T(8,128)(2,1)}), bf16[64,24,360]{2,1,0:T(8,128)(2,1)S(1)}, u32[]{:S(2)}, u32[]{:S(2)}) %all-to-all-start.2) | async-done | bytes 1105952 | tf_op jit(solution)/shard_map/all_to_all | solution.py:223
  (139 shorter events, 55.4 us)
Async XLA Ops:
  6.5 41.9 %copy-start.12 = (f32[16]{0:T(128)S(1)}, f32[16]{0:T(128)}, u32[]{:S(2)}) copy-start(f32[16]{0:T(128)} %param.18) | copy-start | bytes 196
  6.5 43.2 %copy-start.7 = (bf16[128,720]{0,1:T(8,128)(2,1)S(1)}, bf16[128,720]{0,1:T(8,128)(2,1)}, u32[]{:S(2)}) copy-start(bf16[128,720]{0,1:T(8,128)(2,1)} %param.14) | copy-start | bytes 552964
  8.6 42.3 %copy-start.13 = (s32[8]{0:T(128)S(1)}, s32[8]{0:T(128)}, u32[]{:S(2)}) copy-start(s32[8]{0:T(128)} %param.20) | copy-start | bytes 100
  8.6 42.4 %copy-start.14 = (s32[8]{0:T(128)S(1)}, s32[8]{0:T(128)}, u32[]{:S(2)}) copy-start(s32[8]{0:T(128)} %param.19) | copy-start | bytes 100
  8.6 39.8 %all-to-all-start = ((bf16[32,4,16,2,128]{4,2,3,1,0:T(8,128)(2,1)}), bf16[32,4,16,2,128]{4,2,3,1,0:T(8,128)(2,1)S(1)}, u32[]{:S(2)}, u32[]{:S(2)}) async-start(bf16[32,4,16,2,128]{4,2,3,1,0:T(8,128)(2,1)} %broadcast_in_dim.55), calls=%async_computation | async-start | bytes 2097152 | tf_op jit(solution)/shard_map/all_to_all | solution.py:72
  20.3 86.1 %reduce-scatter.3.cloned.1.call-start = ((), (), s32[]{:S(2)}) async-start(), calls=%async_computation.5 | async-start | bytes 921600 | tf_op jit(solution)/shard_map/reduce_scatter | solution.py:138
  48.4 5.8 %copy-start.3 = (bf16[32,4,16,2,128]{4,2,3,1,0:T(8,128)(2,1)}, bf16[32,4,16,2,128]{4,2,3,1,0:T(8,128)(2,1)S(1)}, u32[]{:S(2)}) copy-start(bf16[32,4,16,2,128]{4,2,3,1,0:T(8,128)(2,1)S(1)} %all-to-all-done) | copy-start | bytes 3145732
  48.4 5.8 %collective-permute-start = (bf16[32,4,16,2,128]{4,2,3,1,0:T(8,128)(2,1)S(1)}, bf16[32,4,16,2,128]{4,2,3,1,0:T(8,128)(2,1)}, u32[]{:S(2)}, u32[]{:S(2)}) collective-permute-start(bf16[32,4,16,2,128]{4,2,3,1,0:T(8,128)(2,1)S(1)} %all-to-all-done), channel_id=1, source_target_pairs={{0,4},{4,0},{1,5},{5,1},{2,6},{6,2},{3,7},{7,3},{8,12},{12,8},{9,1... | collective-permute-start | bytes 3145736 | tf_op jit(solution)/shard_map/ppermute | solution.py:73
  70.5 3.1 copy-start.6
  70.5 3.2 copy-start
  75.5 1.9 copy-start.2
  75.5 2.3 copy-start.8
  78.9 5.3 %copy-start.11 = (s32[128,4]{0,1:T(4,128)S(1)}, s32[128,4]{0,1:T(4,128)}, u32[]{:S(2)}) copy-start(s32[128,4]{0,1:T(4,128)} %param.22) | copy-start | bytes 6148
  84.2 115.7 %all-gather.4.cloned.1.call-start = ((), (), s32[]{:S(2)}) async-start(), calls=%async_computation.7 | async-start | bytes 5898240 | tf_op jit(solution)/shard_map/all_gather | solution.py:170
  107.5 41.9 %copy-start.9 = (f32[128,4]{0,1:T(4,128)S(1)}, f32[128,4]{0,1:T(4,128)}, u32[]{:S(2)}) copy-start(f32[128,4]{0,1:T(4,128)} %param.23) | copy-start | bytes 6148
  110.3 90.0 %copy-start.10 = (f32[2880]{0:T(1024)S(1)}, f32[2880]{0:T(1024)}, u32[]{:S(2)}) copy-start(f32[2880]{0:T(1024)} %param.24) | copy-start | bytes 34564
  149.2 177.9 %reduce-scatter.5.cloned.1.call-start = ((), (), s32[]{:S(2)}) async-start(), calls=%async_computation.6 | async-start | bytes 5529600 | tf_op jit(solution)/shard_map/reduce_scatter | solution.py:205
  199.8 76.4 %copy-start.4 = (bf16[64,1,1536]{0,2,1:T(8,128)(2,1)}, bf16[64,1,1536]{0,2,1:T(8,128)(2,1)S(1)}, u32[]{:S(2)}) copy-start(bf16[64,1,1536]{0,2,1:T(8,128)(2,1)S(1)} %copy.130) | copy-start | bytes 589828
  199.9 14.9 %collective-permute-start.1 = (bf16[4,32,24,720]{3,2,1,0:T(8,128)(2,1)}, bf16[4,32,24,720]{3,2,1,0:T(8,128)(2,1)}, u32[]{:S(2)}, u32[]{:S(2)}) collective-permute-start(bf16[4,32,24,720]{3,2,1,0:T(8,128)(2,1)} %bitcast.181), channel_id=1, source_target_pairs={{0,4},{4,0},{1,5},{5,1},{2,6},{6,2},{3,7},{7,3},{8,12},{12,8},{9,1... | collective-permute-start | bytes 13271048 | tf_op jit(solution)/shard_map/ppermute | solution.py:172
  244.5 4.8 %copy-start.1 = (bf16[1536,4,2,360]{0,3,2,1:T(8,128)(2,1)}, bf16[1536,4,2,360]{0,3,2,1:T(8,128)(2,1)S(1)}, u32[]{:S(2)}) copy-start(bf16[1536,4,2,360]{0,3,2,1:T(8,128)(2,1)S(1)} %convolution_convert_fusion) | copy-start | bytes 26542084
  249.3 19.3 %collective-permute-start.2 = (bf16[4,1536,360]{1,2,0:T(8,128)(2,1)}, bf16[4,1536,360]{1,2,0:T(8,128)(2,1)}, u32[]{:S(2)}, u32[]{:S(2)}) collective-permute-start(bf16[4,1536,360]{1,2,0:T(8,128)(2,1)} %dynamic-slice_bitcast_fusion), channel_id=1, source_target_pairs={{0,4},{4,0},{1,5},{5,1},{2,6},{6,2},{3,7},{7,3},{8,12},{12,8},{9,1... | collective-permute-start | bytes 13271048 | tf_op jit(solution)/shard_map/ppermute | solution.py:201
  275.5 0.7 copy-start.15
  331.8 14.8 %copy-start.5 = (bf16[64,1,1536]{0,2,1:T(8,128)(2,1)S(1)}, bf16[64,1,1536]{0,2,1:T(8,128)(2,1)}, u32[]{:S(2)}) copy-start(bf16[64,1,1536]{0,2,1:T(8,128)(2,1)} %copy-done.4) | copy-start | bytes 589828
  333.5 42.1 %all-to-all-start.2 = ((bf16[64,24,360]{2,1,0:T(8,128)(2,1)}), bf16[64,24,360]{2,1,0:T(8,128)(2,1)S(1)}, u32[]{:S(2)}, u32[]{:S(2)}) async-start(bf16[64,24,360]{2,1,0:T(8,128)(2,1)} %gather_fusion.3), calls=%async_computation.4 | async-start | bytes 2359296 | tf_op jit(solution)/shard_map/all_to_all | solution.py:223
Sparse Core Ops, SparseCore 0:
  84.3 22.0 reduce-scatter.2
  149.3 50.4 all-gather.3
  275.6 51.4 reduce-scatter.4
